TPU v7x, 256 devices: a whole 4x4x8 slice. The times are simulated.
256 devices in a mesh: seq: 64 (over x, z, core), ch: 4 (over y).
Axes of the slice: x: 4, y: 4, z: 8, core: 2. Of those that a mesh axis runs over, the one named last changes fastest.
Arguments:
- inputs: bfloat16 [8192, 4096], P('seq'), may hold values from -6 to 6
- norm_gain: float32 [4096], replicated, may hold values from 0.1 to 1.9
- in_weight: bfloat16 [4096, 3, 1024], P('seq', None, 'ch'), may hold values from -0.09375 to 0.09375
- short_filter: float32 [3, 3, 1024], P(None, None, 'ch'), may hold values from -4 to 4
- long_filter: float32 [8192, 1024], P('seq', 'ch'), may hold values from -2.2 to 2.2
- conv_bias: float32 [1024], P('ch'), may hold values from -4 to 4
- out_weight: bfloat16 [1024, 4096], P('ch', 'seq'), may hold values from -0.1875 to 0.1875
- out_grad: bfloat16 [8192, 4096], P('seq'), may hold values from -6 to 6
Outputs:
- block_out: bfloat16 [8192, 4096], P('seq', 'ch')
- in_grad: bfloat16 [8192, 4096], P('seq')
- filter_grad: float32 [8192, 1024], P('seq', 'ch')
All inputs are finite; a program needn't handle non-finite values.
Results may differ from a plain program's by a relative error of at most 0.013.
Values may be sent and summed in bfloat16 or wider, within the bound.
No kernel may reach another device: no remote copies, remote signals or barrier semaphores. Data moves between devices by JAX's collectives and lax.ppermute only.
A program may use at most 64 MiB of HBM per device.

v0:
```python
import math
import jax
import jax.numpy as jnp
from jax import lax
from jax.sharding import PartitionSpec as P

epsilon = 1e-05
highest = lax.Precision.HIGHEST


def passed_along(block, axis, distance):
    devices = range(lax.axis_size(axis))
    route = [(i - distance, i) for i in devices if i - distance in devices]
    return lax.ppermute(block, axis, route)


def regroup(data):
    return lax.all_to_all(data, "seq", split_axis=2, concat_axis=1, tiled=True)


def device_table(devices):
    first = jnp.arange(2 * devices, dtype=jnp.int32)[:, None]
    second = jnp.arange(devices, dtype=jnp.int32)[None, :]
    turns = first * second % (2 * devices)
    phases = 2.0 * math.pi / (2 * devices) * turns.astype(jnp.float32)
    return (jnp.cos(phases), jnp.sin(phases))


def phase_table(devices, place, local_rows, sign):
    total_len = 2 * devices * local_rows
    halves = jnp.arange(2, dtype=jnp.int32)[:, None, None]
    upper = jnp.arange(local_rows, dtype=jnp.int32)[None, :, None]
    lower = jnp.arange(local_rows, dtype=jnp.int32)[None, None, :]
    freqs = 2 * place + halves + 2 * devices * upper
    turns = freqs * lower % total_len
    phases = sign * 2.0 * math.pi / total_len * turns.astype(jnp.float32)
    return (jnp.cos(phases), jnp.sin(phases))


def to_spectrum(signals):
    count = signals.shape[0]
    local_rows = signals.shape[1]
    slab_width = signals.shape[2]
    devices = lax.axis_size("seq")
    place = lax.axis_index("seq")
    share = local_rows // devices
    spread = regroup(signals.reshape(count, 1, local_rows, slab_width))
    cos_dev, sin_dev = device_table(devices)
    real_part = jnp.einsum("kb,ubtc->utkc", cos_dev, spread, precision=highest)
    imag_part = -jnp.einsum("kb,ubtc->utkc", sin_dev, spread, precision=highest)
    joined = jnp.stack([real_part, imag_part], 1).reshape(count * 2, share, 2 * devices, slab_width)
    arrived = regroup(joined).reshape(count, 2, local_rows, 2, slab_width)
    cos_loc, sin_loc = phase_table(devices, place, local_rows, -1.0)
    zero_real = arrived[:, 0]
    zero_imag = arrived[:, 1]
    spec_real = jnp.einsum("ekt,utec->ukec", cos_loc, zero_real, precision=highest) - jnp.einsum(
        "ekt,utec->ukec", sin_loc, zero_imag, precision=highest
    )
    spec_imag = jnp.einsum("ekt,utec->ukec", sin_loc, zero_real, precision=highest) + jnp.einsum(
        "ekt,utec->ukec", cos_loc, zero_imag, precision=highest
    )
    return (spec_real, spec_imag)


def to_signal(spec_real, spec_imag):
    count = spec_real.shape[0]
    local_rows = spec_real.shape[1]
    slab_width = spec_real.shape[3]
    devices = lax.axis_size("seq")
    place = lax.axis_index("seq")
    share = local_rows // devices
    cos_loc, sin_loc = phase_table(devices, place, local_rows, 1.0)
    back_real = jnp.einsum("ekt,ukec->uetc", cos_loc, spec_real, precision=highest) - jnp.einsum(
        "ekt,ukec->uetc", sin_loc, spec_imag, precision=highest
    )
    back_imag = jnp.einsum("ekt,ukec->uetc", sin_loc, spec_real, precision=highest) + jnp.einsum(
        "ekt,ukec->uetc", cos_loc, spec_imag, precision=highest
    )
    joined = jnp.stack([back_real, back_imag], 1).reshape(count * 2, 2, local_rows, slab_width)
    arrived = regroup(joined).reshape(count, 2, 2 * devices, share, slab_width)
    cos_dev, sin_dev = device_table(devices)
    signal = jnp.einsum("kb,uktc->utbc", cos_dev, arrived[:, 0], precision=highest) - jnp.einsum(
        "kb,uktc->utbc", sin_dev, arrived[:, 1], precision=highest
    )
    returned = regroup(signal)
    return returned.reshape(count, local_rows, slab_width) / float(2 * devices * local_rows)


def per_device(
    inputs, norm_gain, in_weight, short_filter, long_filter, conv_bias, out_weight, out_grad
):
    local_rows = inputs.shape[0]
    model_width = inputs.shape[1]
    slab_width = long_filter.shape[1]
    taps = short_filter.shape[1]
    wide_inputs = inputs.astype(jnp.float32)
    inv_rms = lax.rsqrt(jnp.mean(wide_inputs * wide_inputs, axis=1, keepdims=True) + epsilon)
    normed = (wide_inputs * inv_rms * norm_gain).astype(jnp.bfloat16)
    in_panel, out_panel = (
        lax.all_gather(in_weight, "seq", axis=0, tiled=True),
        lax.all_gather(out_weight, "seq", axis=1, tiled=True),
    )
    in_flat = in_panel.reshape(model_width, 3 * slab_width)
    projected = jnp.dot(normed, in_flat, preferred_element_type=jnp.float32)
    projected = projected.astype(jnp.bfloat16).reshape(local_rows, 3, slab_width)
    upper_rim = passed_along(projected[local_rows - (taps - 1) :], "seq", 1)
    extended = jnp.concatenate([upper_rim, projected], 0).astype(jnp.float32)
    mixed = jnp.zeros((local_rows, 3, slab_width), jnp.float32)
    for offset in range(taps):
        begin = taps - 1 - offset
        mixed = mixed + short_filter[:, offset, :][None] * extended[begin : begin + local_rows]
    query_br = mixed[:, 0]
    key_br = mixed[:, 1]
    value_br = mixed[:, 2]
    product = key_br * value_br
    spec_real, spec_imag = to_spectrum(jnp.stack([product, long_filter]))
    sig_real, filt_real = (spec_real[0], spec_real[1])
    sig_imag, filt_imag = (spec_imag[0], spec_imag[1])
    conv_real = sig_real * filt_real - sig_imag * filt_imag
    conv_imag = sig_real * filt_imag + sig_imag * filt_real
    conv_out = to_signal(conv_real[None], conv_imag[None])[0]
    biased = conv_out + conv_bias * product
    gated = (query_br * biased).astype(jnp.bfloat16)
    partial_out = jnp.dot(gated, out_panel, preferred_element_type=jnp.float32)
    summed = lax.psum_scatter(
        partial_out.astype(jnp.bfloat16), "ch", scatter_dimension=1, tiled=True
    ).astype(jnp.float32)
    share = summed.shape[1]
    residual = lax.dynamic_slice_in_dim(wide_inputs, lax.axis_index("ch") * share, share, 1)
    block_out = (residual + summed).astype(jnp.bfloat16)
    gate_grad = jnp.dot(out_grad, out_panel.T, preferred_element_type=jnp.float32)
    carried = gate_grad * query_br
    all_real, all_imag = to_spectrum(jnp.stack([product, long_filter, carried]))
    sig_real, filt_real, grad_real = (all_real[0], all_real[1], all_real[2])
    sig_imag, filt_imag, grad_imag = (all_imag[0], all_imag[1], all_imag[2])
    back_real = grad_real * filt_real + grad_imag * filt_imag
    back_imag = grad_imag * filt_real - grad_real * filt_imag
    pair_real = grad_real * sig_real + grad_imag * sig_imag
    pair_imag = grad_imag * sig_real - grad_real * sig_imag
    returned = to_signal(jnp.stack([back_real, pair_real]), jnp.stack([back_imag, pair_imag]))
    back_conv = returned[0]
    filter_grad = returned[1] * float(local_rows * lax.axis_size("seq")) ** (-0.5)
    source_grad = back_conv + conv_bias * carried
    mixed_grad = jnp.stack([gate_grad * biased, source_grad * value_br, source_grad * key_br], 1)
    lower_rim = passed_along(mixed_grad[: taps - 1], "seq", -1)
    extended_back = jnp.concatenate([mixed_grad, lower_rim], 0)
    proj_grad = jnp.zeros((local_rows, 3, slab_width), jnp.float32)
    for offset in range(taps):
        proj_grad = (
            proj_grad
            + short_filter[:, offset, :][None] * extended_back[offset : offset + local_rows]
        )
    proj_grad = proj_grad.astype(jnp.bfloat16).reshape(local_rows, 3 * slab_width)
    partial_grad = jnp.dot(proj_grad, in_flat.T, preferred_element_type=jnp.float32)
    norm_grad = lax.psum(partial_grad, "ch")
    weighted = norm_grad * norm_gain
    inner_term = jnp.mean(weighted * wide_inputs, axis=1, keepdims=True)
    in_grad = (
        out_grad.astype(jnp.float32) + weighted * inv_rms - wide_inputs * inv_rms**3 * inner_term
    ).astype(jnp.bfloat16)
    return (block_out, in_grad, filter_grad)


def solution(mesh):
    return jax.shard_map(
        per_device,
        mesh=mesh,
        in_specs=(
            P("seq", None),
            P(),
            P("seq", None, "ch"),
            P(None, None, "ch"),
            P("seq", "ch"),
            P("ch"),
            P("ch", "seq"),
            P("seq", None),
        ),
        out_specs=(P("seq", "ch"), P("seq", None), P("seq", "ch")),
        check_vma=False,
    )
```

profile of v0, /device:TPU:1, one launch (start us, length us, event | category | flops | bytes accessed | tf_op | source)
XLA Modules:
  0.0 497.8 jit_solution(17033071886096602538)
XLA Ops:
  11.6 83.9 %all-gather.3.cloned.1.call-done = bf16[4096,3,256]{2,0,1:T(8,128)(2,1)} async-done(((bf16[64,3,256]{2,0,1:T(8,128)(2,1)}), bf16[4096,3,256]{2,0,1:T(8,128)(2,1)}) %all-gather.3.cloned.1.call-update) | async-done | bytes 6291472 | tf_op jit(solution)/shard_map/all_gather | solution.py:100
  95.5 8.7 %copy.102 = bf16[4096,3,256]{0,2,1:T(8,128)(2,1)} copy(bf16[4096,3,256]{2,0,1:T(8,128)(2,1)} %all-gather.3.cloned.1.call-done) | data formatting | bytes 12582912 | tf_op jit(solution)/shard_map/all_gather | solution.py:100
  104.2 5.0 %convolution_convert_fusion.1 = bf16[128,768]{1,0:T(8,128)(2,1)S(1)} fusion(bf16[4096,768]{0,1:T(8,128)(2,1)} %bitcast.250, bf16[128,4096]{1,0:T(8,128)(2,1)S(1)} %copy-done, f32[4096]{0:T(1024)S(1)} %copy-done.13, f32[128]{0:T(128)S(1)} %get-tuple-element.27), kind=kOutput, calls=%fused_computation.25 | convolution fusion | flops 807501824 | bytes 7553536 | tf_op jit(solution)/shard_map/dot_general | solution.py:104
  109.2 2.9 collective-permute-start
  114.0 8.4 %all-to-all-start = ((f32[2,1,128,256]{3,0,1,2:T(2,128)}), f32[2,1,128,256]{3,0,1,2:T(2,128)S(1)}, u32[]{:S(2)}, u32[]{:S(2)}) async-start(f32[2,1,128,256]{3,0,1,2:T(2,128)} %copy.106), calls=%async_computation | async-start | bytes 524288 | tf_op jit(solution)/shard_map/all_to_all | solution.py:18
  122.4 50.2 %all-gather.5.cloned.1.call-done = bf16[256,4096]{0,1:T(8,128)(2,1)} async-done(((bf16[256,64]{0,1:T(8,128)(2,1)}), bf16[256,4096]{0,1:T(8,128)(2,1)}) %all-gather.5.cloned.1.call-update) | async-done | bytes 2097168 | tf_op jit(solution)/shard_map/all_gather | solution.py:101
  176.5 6.8 %all-to-all-start.4 = ((f32[3,1,128,256]{3,1,0,2:T(1,128)}), f32[3,1,128,256]{3,1,0,2:T(1,128)}, u32[]{:S(2)}, u32[]{:S(2)}) async-start(f32[3,1,128,256]{3,1,0,2:T(1,128)} %copy.118), calls=%async_computation.5 | async-start | bytes 786432 | tf_op jit(solution)/shard_map/all_to_all | solution.py:18
  187.6 10.2 %all-to-all-done.4 = f32[3,1,128,256]{3,1,0,2:T(1,128)} async-done(((f32[3,1,128,256]{3,1,0,2:T(1,128)}), f32[3,1,128,256]{3,1,0,2:T(1,128)}, u32[]{:S(2)}, u32[]{:S(2)}) %all-to-all-start.4) | async-done | bytes 393248 | tf_op jit(solution)/shard_map/all_to_all | solution.py:18
  197.7 20.1 %all-to-all-start.1 = ((f32[4,2,128,256]{3,1,0,2:T(2,128)}), f32[4,2,128,256]{3,1,0,2:T(2,128)}, u32[]{:S(2)}, u32[]{:S(2)}) async-start(f32[4,2,128,256]{3,1,0,2:T(2,128)} %copy.110), calls=%async_computation.1 | async-start | bytes 2097152 | tf_op jit(solution)/shard_map/all_to_all | solution.py:18
  223.8 3.8 copy.123
  227.6 18.5 %all-to-all-done.1 = f32[4,2,128,256]{3,1,0,2:T(2,128)} async-done(((f32[4,2,128,256]{3,1,0,2:T(2,128)}), f32[4,2,128,256]{3,1,0,2:T(2,128)}, u32[]{:S(2)}, u32[]{:S(2)}) %all-to-all-start.1) | async-done | bytes 1048608 | tf_op jit(solution)/shard_map/all_to_all | solution.py:18
  246.1 6.2 %all-to-all-start.5 = ((f32[6,2,128,256]{3,1,0,2:T(2,128)}), f32[6,2,128,256]{3,1,0,2:T(2,128)S(1)}, u32[]{:S(2)}, u32[]{:S(2)}) async-start(f32[6,2,128,256]{3,1,0,2:T(2,128)} %copy.123), calls=%async_computation.6 | async-start | bytes 3145728 | tf_op jit(solution)/shard_map/all_to_all | solution.py:18
  268.3 23.8 %all-to-all-done.5 = f32[6,2,128,256]{3,1,0,2:T(2,128)S(1)} async-done(((f32[6,2,128,256]{3,1,0,2:T(2,128)}), f32[6,2,128,256]{3,1,0,2:T(2,128)S(1)}, u32[]{:S(2)}, u32[]{:S(2)}) %all-to-all-start.5) | async-done | bytes 1572896 | tf_op jit(solution)/shard_map/all_to_all | solution.py:18
  292.0 6.3 %all-to-all-start.2 = ((f32[2,2,128,256]{3,1,0,2:T(2,128)}), f32[2,2,128,256]{3,1,0,2:T(2,128)}, u32[]{:S(2)}, u32[]{:S(2)}) async-start(f32[2,2,128,256]{3,1,0,2:T(2,128)} %copy.114), calls=%async_computation.2 | async-start | bytes 1048576 | tf_op jit(solution)/shard_map/all_to_all | solution.py:18
  307.3 2.5 fusion.1
  318.1 10.3 %all-to-all-start.6 = ((f32[4,2,128,256]{3,1,0,2:T(2,128)}), f32[4,2,128,256]{3,1,0,2:T(2,128)S(1)}, u32[]{:S(2)}, u32[]{:S(2)}) async-start(f32[4,2,128,256]{3,1,0,2:T(2,128)} %copy.128), calls=%async_computation.7 | async-start | bytes 2097152 | tf_op jit(solution)/shard_map/all_to_all | solution.py:18
  331.7 25.3 %all-to-all-done.6 = f32[4,2,128,256]{3,1,0,2:T(2,128)S(1)} async-done(((f32[4,2,128,256]{3,1,0,2:T(2,128)}), f32[4,2,128,256]{3,1,0,2:T(2,128)S(1)}, u32[]{:S(2)}, u32[]{:S(2)}) %all-to-all-start.6) | async-done | bytes 1048608 | tf_op jit(solution)/shard_map/all_to_all | solution.py:18
  357.0 6.8 %all-to-all-start.3 = ((f32[1,2,64,256]{3,1,0,2:T(2,128)}), f32[1,2,64,256]{3,1,0,2:T(2,128)}, u32[]{:S(2)}, u32[]{:S(2)}) async-start(f32[1,2,64,256]{3,1,0,2:T(2,128)} %copy.117), calls=%async_computation.3 | async-start | bytes 262144 | tf_op jit(solution)/shard_map/all_to_all | solution.py:18
  366.8 7.0 %all-to-all-done.3 = f32[1,2,64,256]{3,1,0,2:T(2,128)} async-done(((f32[1,2,64,256]{3,1,0,2:T(2,128)}), f32[1,2,64,256]{3,1,0,2:T(2,128)}, u32[]{:S(2)}, u32[]{:S(2)}) %all-to-all-start.3) | async-done | bytes 131104 | tf_op jit(solution)/shard_map/all_to_all | solution.py:18
  373.8 5.2 %all-to-all-start.7 = ((f32[2,2,64,256]{3,1,0,2:T(2,128)}), f32[2,2,64,256]{3,1,0,2:T(2,128)}, u32[]{:S(2)}, u32[]{:S(2)}) async-start(f32[2,2,64,256]{3,1,0,2:T(2,128)} %copy.132), calls=%async_computation.8 | async-start | bytes 524288 | tf_op jit(solution)/shard_map/all_to_all | solution.py:18
  382.2 8.6 %all-to-all-done.7 = f32[2,2,64,256]{3,1,0,2:T(2,128)} async-done(((f32[2,2,64,256]{3,1,0,2:T(2,128)}), f32[2,2,64,256]{3,1,0,2:T(2,128)}, u32[]{:S(2)}, u32[]{:S(2)}) %all-to-all-start.7) | async-done | bytes 262176 | tf_op jit(solution)/shard_map/all_to_all | solution.py:18
  405.0 6.5 %convolution_bitcast_fusion = f32[128,4096]{1,0:T(8,128)} fusion(bf16[4096,3,256]{2,0,1:T(8,128)(2,1)} %all-gather.3.cloned.1.call-done, f32[130,3,256]{2,0,1:T(8,128)S(1)} %pad_maximum_fusion.9, f32[3,256]{1,0:T(4,128)S(1)} %get-tuple-element.28, f32[3,256]{1,0:T(4,128)S(1)} %get-tuple-element.29, f32[3,256]{1,0:T(4,128)S(1)} %bitcast.267, ...), kind=kOutput, calls=%fused_computation | convolution fusion | flops 806092800 | bytes 9580544 | tf_op jit(solution)/shard_map/dot_general | solution.py:154
  413.9 5.8 %reduce-scatter.2.cloned.1.call-done = bf16[128,1024]{1,0:T(8,128)(2,1)} async-done(((bf16[128,4096]{1,0:T(8,128)(2,1)}), bf16[128,1024]{1,0:T(8,128)(2,1)}) %reduce-scatter.2.cloned.1.call-update) | async-done | bytes 262160 | tf_op jit(solution)/shard_map/reduce_scatter | solution.py:125
  421.6 65.2 %all-reduce.2.cloned.1.call-done = f32[128,4096]{1,0:T(8,128)} async-done(((f32[128,4096]{1,0:T(8,128)}), f32[128,4096]{1,0:T(8,128)}) %all-reduce.2.cloned.1.call-update) | async-done | bytes 2097168 | tf_op jit(solution)/shard_map/psum | solution.py:155
  (138 shorter events, 85.1 us)
Async XLA Ops:
  7.2 88.3 %all-gather.3.cloned.1.call-start = ((), (), s32[]{:S(2)}) async-start(), calls=%async_computation.9 | async-start | bytes 6389760 | tf_op jit(solution)/shard_map/all_gather | solution.py:100
  7.9 164.7 %all-gather.5.cloned.1.call-start = ((), (), s32[]{:S(2)}) async-start(), calls=%async_computation.10 | async-start | bytes 2129920 | tf_op jit(solution)/shard_map/all_gather | solution.py:101
  10.7 93.5 %copy-start.17 = (f32[128]{0:T(128)}, f32[128]{0:T(128)S(1)}, u32[]{:S(2)}) copy-start(f32[128]{0:T(128)S(1)} %get-tuple-element.27) | copy-start | bytes 1540
  11.5 92.7 %copy-start = (bf16[128,4096]{1,0:T(8,128)(2,1)S(1)}, bf16[128,4096]{1,0:T(8,128)(2,1)}, u32[]{:S(2)}) copy-start(bf16[128,4096]{1,0:T(8,128)(2,1)} %param.8) | copy-start | bytes 3145732
  11.5 92.6 %copy-start.13 = (f32[4096]{0:T(1024)S(1)}, f32[4096]{0:T(1024)}, u32[]{:S(2)}) copy-start(f32[4096]{0:T(1024)} %param.9) | copy-start | bytes 49156
  109.2 3.6 collective-permute-start
  112.4 60.1 %copy-start.4 = (bf16[128,4096]{1,0:T(8,128)(2,1)S(1)}, bf16[128,4096]{1,0:T(8,128)(2,1)}, u32[]{:S(2)}) copy-start(bf16[128,4096]{1,0:T(8,128)(2,1)} %param.15) | copy-start | bytes 3145732
  114.0 61.3 %copy-start.12 = (f32[128,256]{1,0:T(8,128)S(1)}, f32[128,256]{1,0:T(8,128)}, u32[]{:S(2)}) copy-start(f32[128,256]{1,0:T(8,128)} %param.12) | copy-start | bytes 393220
  114.0 62.5 %all-to-all-start = ((f32[2,1,128,256]{3,0,1,2:T(2,128)}), f32[2,1,128,256]{3,0,1,2:T(2,128)S(1)}, u32[]{:S(2)}, u32[]{:S(2)}) async-start(f32[2,1,128,256]{3,0,1,2:T(2,128)} %copy.106), calls=%async_computation | async-start | bytes 524288 | tf_op jit(solution)/shard_map/all_to_all | solution.py:18
  176.5 21.3 %all-to-all-start.4 = ((f32[3,1,128,256]{3,1,0,2:T(1,128)}), f32[3,1,128,256]{3,1,0,2:T(1,128)}, u32[]{:S(2)}, u32[]{:S(2)}) async-start(f32[3,1,128,256]{3,1,0,2:T(1,128)} %copy.118), calls=%async_computation.5 | async-start | bytes 786432 | tf_op jit(solution)/shard_map/all_to_all | solution.py:18
  197.7 48.3 %all-to-all-start.1 = ((f32[4,2,128,256]{3,1,0,2:T(2,128)}), f32[4,2,128,256]{3,1,0,2:T(2,128)}, u32[]{:S(2)}, u32[]{:S(2)}) async-start(f32[4,2,128,256]{3,1,0,2:T(2,128)} %copy.110), calls=%async_computation.1 | async-start | bytes 2097152 | tf_op jit(solution)/shard_map/all_to_all | solution.py:18
  246.1 46.0 %all-to-all-start.5 = ((f32[6,2,128,256]{3,1,0,2:T(2,128)}), f32[6,2,128,256]{3,1,0,2:T(2,128)S(1)}, u32[]{:S(2)}, u32[]{:S(2)}) async-start(f32[6,2,128,256]{3,1,0,2:T(2,128)} %copy.123), calls=%async_computation.6 | async-start | bytes 3145728 | tf_op jit(solution)/shard_map/all_to_all | solution.py:18
  292.0 26.1 %all-to-all-start.2 = ((f32[2,2,128,256]{3,1,0,2:T(2,128)}), f32[2,2,128,256]{3,1,0,2:T(2,128)}, u32[]{:S(2)}, u32[]{:S(2)}) async-start(f32[2,2,128,256]{3,1,0,2:T(2,128)} %copy.114), calls=%async_computation.2 | async-start | bytes 1048576 | tf_op jit(solution)/shard_map/all_to_all | solution.py:18
  318.1 38.9 %all-to-all-start.6 = ((f32[4,2,128,256]{3,1,0,2:T(2,128)}), f32[4,2,128,256]{3,1,0,2:T(2,128)S(1)}, u32[]{:S(2)}, u32[]{:S(2)}) async-start(f32[4,2,128,256]{3,1,0,2:T(2,128)} %copy.128), calls=%async_computation.7 | async-start | bytes 2097152 | tf_op jit(solution)/shard_map/all_to_all | solution.py:18
  357.0 16.8 %all-to-all-start.3 = ((f32[1,2,64,256]{3,1,0,2:T(2,128)}), f32[1,2,64,256]{3,1,0,2:T(2,128)}, u32[]{:S(2)}, u32[]{:S(2)}) async-start(f32[1,2,64,256]{3,1,0,2:T(2,128)} %copy.117), calls=%async_computation.3 | async-start | bytes 262144 | tf_op jit(solution)/shard_map/all_to_all | solution.py:18
  365.9 30.3 %copy-start.1 = (bf16[256,4096]{0,1:T(8,128)(2,1)S(1)}, bf16[256,4096]{0,1:T(8,128)(2,1)}, u32[]{:S(2)}) copy-start(bf16[256,4096]{0,1:T(8,128)(2,1)} %all-gather.5.cloned.1.call-done) | copy-start | bytes 6291460
  373.8 17.1 %all-to-all-start.7 = ((f32[2,2,64,256]{3,1,0,2:T(2,128)}), f32[2,2,64,256]{3,1,0,2:T(2,128)}, u32[]{:S(2)}, u32[]{:S(2)}) async-start(f32[2,2,64,256]{3,1,0,2:T(2,128)} %copy.132), calls=%async_computation.8 | async-start | bytes 524288 | tf_op jit(solution)/shard_map/all_to_all | solution.py:18
  378.9 40.8 %reduce-scatter.2.cloned.1.call-start = ((), (), s32[]{:S(2)}) async-start(), calls=%async_computation.11 | async-start | bytes 1310720 | tf_op jit(solution)/shard_map/reduce_scatter | solution.py:125
  398.0 88.9 %all-reduce.2.cloned.1.call-start = ((), (), s32[]{:S(2)}) async-start(), calls=%async_computation.12 | async-start | bytes 4194304 | tf_op jit(solution)/shard_map/psum | solution.py:155
  400.0 4.9 collective-permute-start.1
  411.6 75.3 %copy-start.14 = (f32[4096]{0:T(1024)S(1)}, f32[4096]{0:T(1024)}, u32[]{:S(2)}) copy-start(f32[4096]{0:T(1024)} %param.9) | copy-start | bytes 49156
  413.9 75.1 %copy-start.5 = (bf16[128,4096]{1,0:T(8,128)(2,1)S(1)}, bf16[128,4096]{1,0:T(8,128)(2,1)}, u32[]{:S(2)}) copy-start(bf16[128,4096]{1,0:T(8,128)(2,1)} %param.15) | copy-start | bytes 3145732
  413.9 75.1 %copy-start.16 = (f32[128]{0:T(128)S(1)}, f32[128]{0:T(128)}, u32[]{:S(2)}) copy-start(f32[128]{0:T(128)} %get-tuple-element.26) | copy-start | bytes 1540
  413.9 75.1 %copy-start.18 = (f32[128]{0:T(128)S(1)}, f32[128]{0:T(128)}, u32[]{:S(2)}) copy-start(f32[128]{0:T(128)} %copy-done.17) | copy-start | bytes 1540
  (9 other events, 56.3 us)
Sparse Core Ops, SparseCore 0:
  10.8 84.6 all-gather.2
  98.3 74.2 all-gather.4
  398.1 21.5 reduce-scatter.1
  422.0 64.8 all-reduce.1
where the time goes:
time: 507 us; the launch traced here: 498 us
  waiting for transfers between devices  303 us (60%)
  starting transfers between devices  75.5 us (15%)
  local copies, waits for them, and re-layouts  43.7 us (9%)
  matrix products  43.5 us (9%)
  other arithmetic  17.6 us (3%)
  between operations  14.7 us (3%)
    all_to_all x8, waiting for transfers between devices, regroup(): return lax.all_to_all(data, 'seq', split_axis=2, concat_axis=1, tiled=True)  93.3 us
    all_gather x1, waiting for transfers between devices, per_device(): lax.all_gather(in_weight, 'seq', axis=0, tiled=True)  83.9 us
    all_to_all x8, starting transfers between devices, regroup(): return lax.all_to_all(data, 'seq', split_axis=2, concat_axis=1, tiled=True)  70 us
    psum x1, waiting for transfers between devices, per_device(): norm_grad = lax.psum(partial_grad, 'ch')  65.2 us
    all_gather x1, waiting for transfers between devices, per_device(): lax.all_gather(out_weight, 'seq', axis=1, tiled=True)  50.2 us
  transfers between devices with their start and end apart: 14, of which 12 were waited for; matrix products, arithmetic and copies ran while one was open for 19% of the time, Pallas kernels for 0%

commit v1 on v0

--- a/solution.py
+++ b/solution.py
@@ -152,7 +152,7 @@
         )
     proj_grad = proj_grad.astype(jnp.bfloat16).reshape(local_rows, 3 * slab_width)
     partial_grad = jnp.dot(proj_grad, in_flat.T, preferred_element_type=jnp.float32)
-    norm_grad = lax.psum(partial_grad, "ch")
+    norm_grad = jnp.sum(lax.all_gather(partial_grad, "ch"), axis=0)
     weighted = norm_grad * norm_gain
     inner_term = jnp.mean(weighted * wide_inputs, axis=1, keepdims=True)
     in_grad = (

time: 507 us -> 531 us (1.047)
  waiting for transfers between devices: 303 us -> 325 us
    all_gather x0 -> x1, waiting for transfers between devices: none -> 86.7 us  [per_device(): norm_grad = jnp.sum(lax.all_gather(partial_grad, 'ch'), axis=0)]
    psum x1 -> x0, waiting for transfers between devices: 65.2 us -> none  [per_device(): norm_grad = lax.psum(partial_grad, 'ch')]
  transfers between devices with their start and end apart: 14 -> 14, of which waited for: 12 -> 12; matrix products, arithmetic and copies ran while one was open for 19% -> 17% of each run, Pallas kernels for 0% -> 0%
where the time goes in v1:
time: 531 us; the launch traced here: 522 us
  waiting for transfers between devices  325 us (61%)
  starting transfers between devices  75.5 us (14%)
  local copies, waits for them, and re-layouts  45.1 us (8%)
  matrix products  43.5 us (8%)
  other arithmetic  18.5 us (3%)
  between operations  14.7 us (3%)
    all_to_all x8, waiting for transfers between devices, regroup(): return lax.all_to_all(data, 'seq', split_axis=2, concat_axis=1, tiled=True)  93.3 us
    all_gather x1, waiting for transfers between devices, per_device(): norm_grad = jnp.sum(lax.all_gather(partial_grad, 'ch'), axis=0)  86.7 us
    all_gather x1, waiting for transfers between devices, per_device(): lax.all_gather(in_weight, 'seq', axis=0, tiled=True)  83.9 us
    all_to_all x8, starting transfers between devices, regroup(): return lax.all_to_all(data, 'seq', split_axis=2, concat_axis=1, tiled=True)  70 us
    all_gather x1, waiting for transfers between devices, per_device(): lax.all_gather(out_weight, 'seq', axis=1, tiled=True)  50.2 us
  transfers between devices with their start and end apart: 14, of which 12 were waited for; matrix products, arithmetic and copies ran while one was open for 17% of the time, Pallas kernels for 0%

profile of v1, /device:TPU:1, one launch (start us, length us, event | category | flops | bytes accessed | tf_op | source)
XLA Modules:
  0.0 522.2 jit_solution(1868952347212673070)
XLA Ops:
  11.6 83.9 %all-gather.5.cloned.1.call-done = bf16[4096,3,256]{2,0,1:T(8,128)(2,1)} async-done(((bf16[64,3,256]{2,0,1:T(8,128)(2,1)}), bf16[4096,3,256]{2,0,1:T(8,128)(2,1)}) %all-gather.5.cloned.1.call-update) | async-done | bytes 6291472 | tf_op jit(solution)/shard_map/all_gather | solution.py:100
  95.5 8.7 %copy.102 = bf16[4096,3,256]{0,2,1:T(8,128)(2,1)} copy(bf16[4096,3,256]{2,0,1:T(8,128)(2,1)} %all-gather.5.cloned.1.call-done) | data formatting | bytes 12582912 | tf_op jit(solution)/shard_map/all_gather | solution.py:100
  104.2 5.0 convolution_convert_fusion.1
  109.2 2.9 collective-permute-start
  114.0 8.4 %all-to-all-start = ((f32[2,1,128,256]{3,0,1,2:T(2,128)}), f32[2,1,128,256]{3,0,1,2:T(2,128)S(1)}, u32[]{:S(2)}, u32[]{:S(2)}) async-start(f32[2,1,128,256]{3,0,1,2:T(2,128)} %copy.106), calls=%async_computation | async-start | bytes 524288 | tf_op jit(solution)/shard_map/all_to_all | solution.py:18
  122.4 50.2 %all-gather.7.cloned.1.call-done = bf16[256,4096]{0,1:T(8,128)(2,1)} async-done(((bf16[256,64]{0,1:T(8,128)(2,1)}), bf16[256,4096]{0,1:T(8,128)(2,1)}) %all-gather.7.cloned.1.call-update) | async-done | bytes 2097168 | tf_op jit(solution)/shard_map/all_gather | solution.py:101
  176.5 6.8 %all-to-all-start.4 = ((f32[3,1,128,256]{3,1,0,2:T(1,128)}), f32[3,1,128,256]{3,1,0,2:T(1,128)}, u32[]{:S(2)}, u32[]{:S(2)}) async-start(f32[3,1,128,256]{3,1,0,2:T(1,128)} %copy.118), calls=%async_computation.5 | async-start | bytes 786432 | tf_op jit(solution)/shard_map/all_to_all | solution.py:18
  187.6 10.2 %all-to-all-done.4 = f32[3,1,128,256]{3,1,0,2:T(1,128)} async-done(((f32[3,1,128,256]{3,1,0,2:T(1,128)}), f32[3,1,128,256]{3,1,0,2:T(1,128)}, u32[]{:S(2)}, u32[]{:S(2)}) %all-to-all-start.4) | async-done | bytes 393248 | tf_op jit(solution)/shard_map/all_to_all | solution.py:18
  197.7 20.1 %all-to-all-start.1 = ((f32[4,2,128,256]{3,1,0,2:T(2,128)}), f32[4,2,128,256]{3,1,0,2:T(2,128)}, u32[]{:S(2)}, u32[]{:S(2)}) async-start(f32[4,2,128,256]{3,1,0,2:T(2,128)} %copy.110), calls=%async_computation.1 | async-start | bytes 2097152 | tf_op jit(solution)/shard_map/all_to_all | solution.py:18
  223.8 3.8 copy.123
  227.6 18.5 %all-to-all-done.1 = f32[4,2,128,256]{3,1,0,2:T(2,128)} async-done(((f32[4,2,128,256]{3,1,0,2:T(2,128)}), f32[4,2,128,256]{3,1,0,2:T(2,128)}, u32[]{:S(2)}, u32[]{:S(2)}) %all-to-all-start.1) | async-done | bytes 1048608 | tf_op jit(solution)/shard_map/all_to_all | solution.py:18
  246.1 6.2 %all-to-all-start.5 = ((f32[6,2,128,256]{3,1,0,2:T(2,128)}), f32[6,2,128,256]{3,1,0,2:T(2,128)S(1)}, u32[]{:S(2)}, u32[]{:S(2)}) async-start(f32[6,2,128,256]{3,1,0,2:T(2,128)} %copy.123), calls=%async_computation.6 | async-start | bytes 3145728 | tf_op jit(solution)/shard_map/all_to_all | solution.py:18
  268.2 23.8 %all-to-all-done.5 = f32[6,2,128,256]{3,1,0,2:T(2,128)S(1)} async-done(((f32[6,2,128,256]{3,1,0,2:T(2,128)}), f32[6,2,128,256]{3,1,0,2:T(2,128)S(1)}, u32[]{:S(2)}, u32[]{:S(2)}) %all-to-all-start.5) | async-done | bytes 1572896 | tf_op jit(solution)/shard_map/all_to_all | solution.py:18
  292.0 6.3 %all-to-all-start.2 = ((f32[2,2,128,256]{3,1,0,2:T(2,128)}), f32[2,2,128,256]{3,1,0,2:T(2,128)}, u32[]{:S(2)}, u32[]{:S(2)}) async-start(f32[2,2,128,256]{3,1,0,2:T(2,128)} %copy.114), calls=%async_computation.2 | async-start | bytes 1048576 | tf_op jit(solution)/shard_map/all_to_all | solution.py:18
  318.1 10.3 %all-to-all-start.6 = ((f32[4,2,128,256]{3,1,0,2:T(2,128)}), f32[4,2,128,256]{3,1,0,2:T(2,128)S(1)}, u32[]{:S(2)}, u32[]{:S(2)}) async-start(f32[4,2,128,256]{3,1,0,2:T(2,128)} %copy.128), calls=%async_computation.7 | async-start | bytes 2097152 | tf_op jit(solution)/shard_map/all_to_all | solution.py:18
  331.7 25.3 %all-to-all-done.6 = f32[4,2,128,256]{3,1,0,2:T(2,128)S(1)} async-done(((f32[4,2,128,256]{3,1,0,2:T(2,128)}), f32[4,2,128,256]{3,1,0,2:T(2,128)S(1)}, u32[]{:S(2)}, u32[]{:S(2)}) %all-to-all-start.6) | async-done | bytes 1048608 | tf_op jit(solution)/shard_map/all_to_all | solution.py:18
  357.0 6.8 %all-to-all-start.3 = ((f32[1,2,64,256]{3,1,0,2:T(2,128)}), f32[1,2,64,256]{3,1,0,2:T(2,128)}, u32[]{:S(2)}, u32[]{:S(2)}) async-start(f32[1,2,64,256]{3,1,0,2:T(2,128)} %copy.117), calls=%async_computation.3 | async-start | bytes 262144 | tf_op jit(solution)/shard_map/all_to_all | solution.py:18
  366.8 7.0 %all-to-all-done.3 = f32[1,2,64,256]{3,1,0,2:T(2,128)} async-done(((f32[1,2,64,256]{3,1,0,2:T(2,128)}), f32[1,2,64,256]{3,1,0,2:T(2,128)}, u32[]{:S(2)}, u32[]{:S(2)}) %all-to-all-start.3) | async-done | bytes 131104 | tf_op jit(solution)/shard_map/all_to_all | solution.py:18
  373.8 5.2 all-to-all-start.7
  382.3 8.6 %all-to-all-done.7 = f32[2,2,64,256]{3,1,0,2:T(2,128)} async-done(((f32[2,2,64,256]{3,1,0,2:T(2,128)}), f32[2,2,64,256]{3,1,0,2:T(2,128)}, u32[]{:S(2)}, u32[]{:S(2)}) %all-to-all-start.7) | async-done | bytes 262176 | tf_op jit(solution)/shard_map/all_to_all | solution.py:18
  405.0 6.5 %convolution_bitcast_fusion = f32[128,4096]{1,0:T(8,128)} fusion(bf16[4096,3,256]{2,0,1:T(8,128)(2,1)} %all-gather.5.cloned.1.call-done, f32[130,3,256]{2,0,1:T(8,128)S(1)} %pad_maximum_fusion.9, f32[3,256]{1,0:T(4,128)S(1)} %get-tuple-element.28, f32[3,256]{1,0:T(4,128)S(1)} %get-tuple-element.29, f32[3,256]{1,0:T(4,128)S(1)} %bitcast.269, ...), kind=kOutput, calls=%fused_computation | convolution fusion | flops 806092800 | bytes 9580544 | tf_op jit(solution)/shard_map/dot_general | solution.py:154
  413.2 6.6 %reduce-scatter.2.cloned.1.call-done = bf16[128,1024]{1,0:T(8,128)(2,1)} async-done(((bf16[128,4096]{1,0:T(8,128)(2,1)}), bf16[128,1024]{1,0:T(8,128)(2,1)}) %reduce-scatter.2.cloned.1.call-update) | async-done | bytes 262160 | tf_op jit(solution)/shard_map/reduce_scatter | solution.py:125
  421.5 86.7 %all-gather.9.cloned.1.call-done = f32[512,4096]{1,0:T(8,128)} async-done(((f32[128,4096]{1,0:T(8,128)}), f32[512,4096]{1,0:T(8,128)}) %all-gather.9.cloned.1.call-update) | async-done | bytes 8388624 | tf_op jit(solution)/shard_map/all_gather | solution.py:155
  508.2 4.2 reduce_sum.28
  (137 shorter events, 85.8 us)
Async XLA Ops:
  7.2 88.3 %all-gather.5.cloned.1.call-start = ((), (), s32[]{:S(2)}) async-start(), calls=%async_computation.9 | async-start | bytes 6389760 | tf_op jit(solution)/shard_map/all_gather | solution.py:100
  7.9 164.7 %all-gather.7.cloned.1.call-start = ((), (), s32[]{:S(2)}) async-start(), calls=%async_computation.10 | async-start | bytes 2129920 | tf_op jit(solution)/shard_map/all_gather | solution.py:101
  10.7 93.5 %copy-start.16 = (f32[128]{0:T(128)}, f32[128]{0:T(128)S(1)}, u32[]{:S(2)}) copy-start(f32[128]{0:T(128)S(1)} %get-tuple-element.27) | copy-start | bytes 1540
  11.6 92.6 %copy-start = (bf16[128,4096]{1,0:T(8,128)(2,1)S(1)}, bf16[128,4096]{1,0:T(8,128)(2,1)}, u32[]{:S(2)}) copy-start(bf16[128,4096]{1,0:T(8,128)(2,1)} %param.8) | copy-start | bytes 3145732
  11.6 92.6 %copy-start.12 = (f32[4096]{0:T(1024)S(1)}, f32[4096]{0:T(1024)}, u32[]{:S(2)}) copy-start(f32[4096]{0:T(1024)} %param.9) | copy-start | bytes 49156
  109.2 3.6 collective-permute-start
  112.4 60.1 %copy-start.3 = (bf16[128,4096]{1,0:T(8,128)(2,1)S(1)}, bf16[128,4096]{1,0:T(8,128)(2,1)}, u32[]{:S(2)}) copy-start(bf16[128,4096]{1,0:T(8,128)(2,1)} %param.15) | copy-start | bytes 3145732
  114.0 61.3 %copy-start.11 = (f32[128,256]{1,0:T(8,128)S(1)}, f32[128,256]{1,0:T(8,128)}, u32[]{:S(2)}) copy-start(f32[128,256]{1,0:T(8,128)} %param.12) | copy-start | bytes 393220
  114.0 62.5 %all-to-all-start = ((f32[2,1,128,256]{3,0,1,2:T(2,128)}), f32[2,1,128,256]{3,0,1,2:T(2,128)S(1)}, u32[]{:S(2)}, u32[]{:S(2)}) async-start(f32[2,1,128,256]{3,0,1,2:T(2,128)} %copy.106), calls=%async_computation | async-start | bytes 524288 | tf_op jit(solution)/shard_map/all_to_all | solution.py:18
  176.5 21.3 %all-to-all-start.4 = ((f32[3,1,128,256]{3,1,0,2:T(1,128)}), f32[3,1,128,256]{3,1,0,2:T(1,128)}, u32[]{:S(2)}, u32[]{:S(2)}) async-start(f32[3,1,128,256]{3,1,0,2:T(1,128)} %copy.118), calls=%async_computation.5 | async-start | bytes 786432 | tf_op jit(solution)/shard_map/all_to_all | solution.py:18
  197.7 48.3 %all-to-all-start.1 = ((f32[4,2,128,256]{3,1,0,2:T(2,128)}), f32[4,2,128,256]{3,1,0,2:T(2,128)}, u32[]{:S(2)}, u32[]{:S(2)}) async-start(f32[4,2,128,256]{3,1,0,2:T(2,128)} %copy.110), calls=%async_computation.1 | async-start | bytes 2097152 | tf_op jit(solution)/shard_map/all_to_all | solution.py:18
  246.1 46.0 %all-to-all-start.5 = ((f32[6,2,128,256]{3,1,0,2:T(2,128)}), f32[6,2,128,256]{3,1,0,2:T(2,128)S(1)}, u32[]{:S(2)}, u32[]{:S(2)}) async-start(f32[6,2,128,256]{3,1,0,2:T(2,128)} %copy.123), calls=%async_computation.6 | async-start | bytes 3145728 | tf_op jit(solution)/shard_map/all_to_all | solution.py:18
  292.0 26.1 %all-to-all-start.2 = ((f32[2,2,128,256]{3,1,0,2:T(2,128)}), f32[2,2,128,256]{3,1,0,2:T(2,128)}, u32[]{:S(2)}, u32[]{:S(2)}) async-start(f32[2,2,128,256]{3,1,0,2:T(2,128)} %copy.114), calls=%async_computation.2 | async-start | bytes 1048576 | tf_op jit(solution)/shard_map/all_to_all | solution.py:18
  318.1 38.9 %all-to-all-start.6 = ((f32[4,2,128,256]{3,1,0,2:T(2,128)}), f32[4,2,128,256]{3,1,0,2:T(2,128)S(1)}, u32[]{:S(2)}, u32[]{:S(2)}) async-start(f32[4,2,128,256]{3,1,0,2:T(2,128)} %copy.128), calls=%async_computation.7 | async-start | bytes 2097152 | tf_op jit(solution)/shard_map/all_to_all | solution.py:18
  357.0 16.8 %all-to-all-start.3 = ((f32[1,2,64,256]{3,1,0,2:T(2,128)}), f32[1,2,64,256]{3,1,0,2:T(2,128)}, u32[]{:S(2)}, u32[]{:S(2)}) async-start(f32[1,2,64,256]{3,1,0,2:T(2,128)} %copy.117), calls=%async_computation.3 | async-start | bytes 262144 | tf_op jit(solution)/shard_map/all_to_all | solution.py:18
  365.3 29.1 %copy-start.14 = (f32[256]{0:T(256)S(1)}, f32[256]{0:T(256)}, u32[]{:S(2)}) copy-start(f32[256]{0:T(256)} %param.13) | copy-start | bytes 3076
  365.9 30.3 %copy-start.1 = (bf16[256,4096]{0,1:T(8,128)(2,1)S(1)}, bf16[256,4096]{0,1:T(8,128)(2,1)}, u32[]{:S(2)}) copy-start(bf16[256,4096]{0,1:T(8,128)(2,1)} %all-gather.7.cloned.1.call-done) | copy-start | bytes 6291460
  373.8 17.1 %all-to-all-start.7 = ((f32[2,2,64,256]{3,1,0,2:T(2,128)}), f32[2,2,64,256]{3,1,0,2:T(2,128)}, u32[]{:S(2)}, u32[]{:S(2)}) async-start(f32[2,2,64,256]{3,1,0,2:T(2,128)} %copy.132), calls=%async_computation.8 | async-start | bytes 524288 | tf_op jit(solution)/shard_map/all_to_all | solution.py:18
  378.9 40.8 %reduce-scatter.2.cloned.1.call-start = ((), (), s32[]{:S(2)}) async-start(), calls=%async_computation.11 | async-start | bytes 1310720 | tf_op jit(solution)/shard_map/reduce_scatter | solution.py:125
  398.0 7.0 %copy-start.6 = (f32[128,1,256]{2,0,1:T(8,128)S(1)}, f32[128,1,256]{2,0,1:T(8,128)}, u32[]{:S(2)}) copy-start(f32[128,1,256]{2,0,1:T(8,128)} %get-tuple-element.5) | copy-start | bytes 393220
  398.0 7.0 %copy-start.7 = (f32[128,1,256]{2,0,1:T(8,128)S(1)}, f32[128,1,256]{2,0,1:T(8,128)}, u32[]{:S(2)}) copy-start(f32[128,1,256]{2,0,1:T(8,128)} %get-tuple-element.19) | copy-start | bytes 393220
  398.0 110.1 %all-gather.9.cloned.1.call-start = ((), (), s32[]{:S(2)}) async-start(), calls=%async_computation.12 | async-start | bytes 10485760 | tf_op jit(solution)/shard_map/all_gather | solution.py:155
  400.0 4.9 collective-permute-start.1
  508.2 4.2 copy-start.13
  (8 other events, 13.9 us)
Sparse Core Ops, SparseCore 0:
  10.8 84.6 all-gather.4
  98.3 74.2 all-gather.6
  398.1 21.5 reduce-scatter.1
  421.4 86.7 all-gather.8
